TPU v7x, 512 devices: a whole 4x4x16 slice. The times are simulated.
512 devices in a mesh: dp: 8 (over x, y_hi), expert: 64 (over y_lo, z, core).
Axes of the slice: x: 4, y: 4 (y_hi: 2, y_lo: 2; y = y_hi * 2 + y_lo), z: 16, core: 2. Of those that a mesh axis runs over, the one named last changes fastest.
Arguments:
- tokens: bfloat16 [65536, 2048], P(('dp', 'expert')), may hold values from -6 to 6
- out_grad: bfloat16 [65536, 2048], P(('dp', 'expert')), may hold values from -6 to 6
- combine: float32 [65536, 2], P(('dp', 'expert')), may hold values from 0.1 to 1
- expert_ids: int32 [65536, 2], P(('dp', 'expert')), may hold values from 0 to 63, all different within a row; in each aligned block of 128 rows (0 to 127, 128 to 255, ...) at most 5 rows name the same one
- gate_weight: bfloat16 [64, 2048, 768], P('expert', 'dp'), may hold values from -0.125 to 0.125
- up_weight: bfloat16 [64, 2048, 768], P('expert', 'dp'), may hold values from -0.125 to 0.125
- down_weight: bfloat16 [64, 2048, 768], P('expert', 'dp'), may hold values from -0.21875 to 0.21875
Outputs:
- token_grad: bfloat16 [65536, 2048], P(('dp', 'expert'))
- down_grad: bfloat16 [64, 2048, 768], P('expert', 'dp')
Inputs may be any that keep to these rules, and one draw needn't show every extreme that they name: `expert_ids`: each row names 2 different experts. Among the 128 rows of one device no expert is named more than 5 times, a bound that some block reaches.
All inputs are finite; a program needn't handle non-finite values.
Results may differ from a plain program's by a relative error of at most 0.012.
Values may be sent and summed in bfloat16 or wider, within the bound.
No kernel may reach another device: no remote copies, remote signals or barrier semaphores. Data moves between devices by JAX's collectives and lax.ppermute only.
A program may use at most 64 MiB of HBM per device.

v0:
```python
import jax
import jax.numpy as jnp
from jax import lax
from jax.sharding import Mesh
from jax.sharding import PartitionSpec as P

TOP = 2
CAP = 5
SUB = ("ylo", "z", "core")
ROWS = ("dp",) + SUB


def local_then_z(x, kinds):
    x = lax.all_to_all(x, "core", 3, 3, tiled=True)
    x = lax.all_to_all(x, "ylo", 1, 1, tiled=True)
    return [lax.all_to_all(x[k], "z", 1, 1, tiled=True) for k in range(kinds)]


def z_then_local(x):
    x = lax.all_to_all(x, "z", 1, 1, tiled=True)
    x = lax.all_to_all(x, "ylo", 0, 0, tiled=True)
    return lax.all_to_all(x, "core", 2, 2, tiled=True)


def body(tokens, out_grad, combine, expert_ids, gate_weight, up_weight, down_weight):
    token_rows = tokens.shape[0]
    width = tokens.shape[1]
    n_ylo, n_z, n_core = (lax.axis_size(a) for a in SUB)
    expert_count = n_ylo * n_z * n_core
    capacity = CAP
    positions = expert_count * capacity
    w_gate = lax.all_gather(gate_weight, "dp", axis=1, tiled=True)[0]
    w_up = lax.all_gather(up_weight, "dp", axis=1, tiled=True)[0]
    w_down = lax.all_gather(down_weight, "dp", axis=1, tiled=True)[0]
    flat_ids = expert_ids.reshape(-1)
    onehot = (flat_ids[:, None] == jnp.arange(expert_count, dtype=jnp.int32)[None, :]).astype(
        jnp.int32
    )
    earlier = jnp.cumsum(onehot, axis=0) - onehot
    slot_index = jnp.sum(earlier * onehot, axis=1)
    target = flat_ids * capacity + slot_index
    matches = target[None, :] == jnp.arange(positions, dtype=jnp.int32)[:, None]
    picker = jnp.sum(
        matches.reshape(positions, token_rows, TOP).astype(jnp.float32), axis=2
    ).astype(jnp.bfloat16)
    slot_weight = jnp.sum(
        jnp.where(matches, combine.reshape(-1)[None, :], jnp.float32(0.0)), axis=1
    )
    row_send = jnp.dot(picker, tokens, preferred_element_type=jnp.float32).astype(jnp.bfloat16)
    picked_grad = jnp.dot(picker, out_grad, preferred_element_type=jnp.float32)
    grad_send = (slot_weight[:, None] * picked_grad).astype(jnp.bfloat16)
    send = jnp.stack([row_send, grad_send]).reshape(2, n_ylo, n_z, n_core, capacity, width)
    rows_in, grads_in = local_then_z(send, 2)
    rows_in = rows_in.reshape(positions, width)
    grads_in = grads_in.reshape(positions, width)
    gate_pre = jnp.dot(rows_in, w_gate, preferred_element_type=jnp.float32)
    up_pre = jnp.dot(rows_in, w_up, preferred_element_type=jnp.float32)
    sigmoid_gate = jax.nn.sigmoid(gate_pre)
    silu_gate = gate_pre * sigmoid_gate
    hidden = (silu_gate * up_pre).astype(jnp.bfloat16)
    hidden_grad = jnp.dot(grads_in, w_down, preferred_element_type=jnp.float32)
    gate_grad = (
        hidden_grad * up_pre * sigmoid_gate * (1.0 + gate_pre * (1.0 - sigmoid_gate))
    ).astype(jnp.bfloat16)
    up_grad = (hidden_grad * silu_gate).astype(jnp.bfloat16)
    contract_hidden = (((1,), (1,)), ((), ()))
    row_grad = (
        lax.dot_general(gate_grad, w_gate, contract_hidden, preferred_element_type=jnp.float32)
        + lax.dot_general(up_grad, w_up, contract_hidden, preferred_element_type=jnp.float32)
    ).astype(jnp.bfloat16)
    back_rows = z_then_local(row_grad.reshape(n_ylo, n_z, n_core, capacity, width))
    token_grad = lax.dot_general(
        picker,
        back_rows.reshape(positions, width),
        (((0,), (0,)), ((), ())),
        preferred_element_type=jnp.float32,
    ).astype(jnp.bfloat16)
    down_grad = lax.psum_scatter(
        lax.dot_general(
            grads_in, hidden, (((0,), (0,)), ((), ())), preferred_element_type=jnp.float32
        ).astype(jnp.bfloat16),
        "dp",
        scatter_dimension=0,
        tiled=True,
    )
    return (token_grad, down_grad[None])


def solution(mesh):
    n_dp, n_expert = mesh.devices.shape
    fine = Mesh(mesh.devices.reshape(n_dp, 2, n_expert // 4, 2), ("dp",) + SUB)
    rows = P(ROWS, None)
    weights = P(SUB, "dp", None)
    return jax.shard_map(
        body,
        mesh=fine,
        in_specs=(rows, rows, rows, rows, weights, weights, weights),
        out_specs=(rows, weights),
        check_vma=False,
    )
```

profile of v0, /device:TPU:33, one launch (start us, length us, event | category | flops | bytes accessed | tf_op | source)
XLA Modules:
  0.0 378.4 jit_solution(1346013559021178343)
XLA Ops:
  13.6 2.4 stack.10
  17.6 3.4 stack.9
  21.0 2.5 pad_maximum_fusion
  25.3 6.1 %all_to_all.35 = bf16[2,2,16,2,5,2048]{5,2,4,1,0,3:T(8,128)(2,1)S(1)} all-to-all(bf16[2,2,16,2,5,2048]{5,2,4,1,0,3:T(8,128)(2,1)S(1)} %copy.54), channel_id=1, replica_groups=mesh['dp'=8,'ylo'=2,'z'=16,'core'=2] {'core'}, dimensions={3} | all-to-all | bytes 5242880 | tf_op jit(solution)/shard_map/all_to_all | solution.py:14
  31.8 38.4 %all_to_all.36 = bf16[2,2,16,2,5,2048]{5,2,4,3,0,1:T(8,128)(2,1)S(1)} all-to-all(bf16[2,2,16,2,5,2048]{5,2,4,3,0,1:T(8,128)(2,1)S(1)} %copy.55), channel_id=1, replica_groups=mesh['dp'=8,'ylo'=2,'z'=16,'core'=2] {'ylo'}, dimensions={1} | all-to-all | bytes 5242880 | tf_op jit(solution)/shard_map/all_to_all | solution.py:15
  70.4 2.4 copy.58
  72.8 12.2 %all-to-all-start.3 = ((bf16[2,16,2,5,2048]{4,2,3,0,1:T(2,128)(2,1)}), bf16[2,16,2,5,2048]{4,2,3,0,1:T(2,128)(2,1)S(1)}, u32[]{:S(2)}, u32[]{:S(2)}) async-start(bf16[2,16,2,5,2048]{4,2,3,0,1:T(2,128)(2,1)} %copy.58), calls=%async_computation.3 | async-start | bytes 2621440 | tf_op jit(solution)/shard_map/all_to_all | solution.py:16
  85.7 2.4 copy.56
  88.1 53.9 %all-to-all-done.3 = bf16[2,16,2,5,2048]{4,2,3,0,1:T(2,128)(2,1)S(1)} async-done(((bf16[2,16,2,5,2048]{4,2,3,0,1:T(2,128)(2,1)}), bf16[2,16,2,5,2048]{4,2,3,0,1:T(2,128)(2,1)S(1)}, u32[]{:S(2)}, u32[]{:S(2)}) %all-to-all-start.3) | async-done | bytes 1310752 | tf_op jit(solution)/shard_map/all_to_all | solution.py:16
  142.0 12.2 %all-to-all-start.2 = ((bf16[2,16,2,5,2048]{4,2,3,0,1:T(2,128)(2,1)}), bf16[2,16,2,5,2048]{4,2,3,0,1:T(2,128)(2,1)}, u32[]{:S(2)}, u32[]{:S(2)}) async-start(bf16[2,16,2,5,2048]{4,2,3,0,1:T(2,128)(2,1)} %copy.56), calls=%async_computation.2 | async-start | bytes 2621440 | tf_op jit(solution)/shard_map/all_to_all | solution.py:16
  155.2 2.0 copy.59
  158.7 52.2 %all-to-all-done.2 = bf16[2,16,2,5,2048]{4,2,3,0,1:T(2,128)(2,1)} async-done(((bf16[2,16,2,5,2048]{4,2,3,0,1:T(2,128)(2,1)}), bf16[2,16,2,5,2048]{4,2,3,0,1:T(2,128)(2,1)}, u32[]{:S(2)}, u32[]{:S(2)}) %all-to-all-start.2) | async-done | bytes 1310752 | tf_op jit(solution)/shard_map/all_to_all | solution.py:16
  210.8 2.0 copy.57
  214.3 4.6 %fusion.2 = f32[320,768]{1,0:T(8,128)} fusion(bf16[320,2048]{1,0:T(8,128)(2,1)} %reshape.61, bf16[1,2048,768]{2,1,0:T(8,128)(2,1)} %all-gather.8.cloned.1.call-done), kind=kOutput, calls=%fused_computation.4 | convolution fusion | flops 1006632960 | bytes 5439488 | tf_op jit(solution)/shard_map/dot_general | solution.py:56
  218.9 3.2 fusion.6
  223.1 3.6 convolution_convert_fusion
  226.7 29.6 %all-gather.4.cloned.1.call-done = bf16[1,2048,768]{2,1,0:T(8,128)(2,1)} async-done(((bf16[1,256,768]{2,1,0:T(8,128)(2,1)}), bf16[1,2048,768]{2,1,0:T(8,128)(2,1)}) %all-gather.4.cloned.1.call-update) | async-done | bytes 3145744 | tf_op jit(solution)/shard_map/all_gather | solution.py:34
  256.3 3.2 fusion.8
  261.4 2.3 fusion.13
  263.7 2.4 reshape.62
  267.6 74.4 %all_to_all.37 = bf16[2,16,2,5,2048]{4,2,3,0,1:T(2,128)(2,1)S(1)} all-to-all(bf16[2,16,2,5,2048]{4,2,3,0,1:T(2,128)(2,1)S(1)} %copy.60), channel_id=1, replica_groups=mesh['dp'=8,'ylo'=2,'z'=16,'core'=2] {'z'}, dimensions={1} | all-to-all | bytes 2621440 | tf_op jit(solution)/shard_map/all_to_all | solution.py:20
  342.7 17.1 %all_to_all.38 = bf16[2,16,2,5,2048]{4,1,3,2,0:T(8,128)(2,1)S(1)} all-to-all(bf16[2,16,2,5,2048]{4,1,3,2,0:T(8,128)(2,1)S(1)} %copy.61), channel_id=1, replica_groups=mesh['dp'=8,'ylo'=2,'z'=16,'core'=2] {'ylo'}, dimensions={0} | all-to-all | bytes 2621440 | tf_op jit(solution)/shard_map/all_to_all | solution.py:21
  360.0 7.2 %all_to_all.39 = bf16[2,16,2,5,2048]{4,1,3,0,2:T(8,128)(2,1)S(1)} all-to-all(bf16[2,16,2,5,2048]{4,1,3,0,2:T(8,128)(2,1)S(1)} %copy.62), channel_id=1, replica_groups=mesh['dp'=8,'ylo'=2,'z'=16,'core'=2] {'core'}, dimensions={2} | all-to-all | bytes 2621440 | tf_op jit(solution)/shard_map/all_to_all | solution.py:22
  369.3 2.6 convolution_convert_fusion.2
  (65 shorter events, 22.2 us)
Async XLA Ops:
  7.2 4.8 %copy-start = (bf16[128,2048]{1,0:T(8,128)(2,1)S(1)}, bf16[128,2048]{1,0:T(8,128)(2,1)}, u32[]{:S(2)}) copy-start(bf16[128,2048]{1,0:T(8,128)(2,1)} %param.8) | copy-start | bytes 1572868
  7.2 207.1 %all-gather.8.cloned.1.call-start = ((), (), s32[]{:S(2)}) async-start(), calls=%async_computation.10 | async-start | bytes 3538944 | tf_op jit(solution)/shard_map/all_gather | solution.py:32
  13.6 2.4 copy-start.5
  72.8 69.2 %all-to-all-start.3 = ((bf16[2,16,2,5,2048]{4,2,3,0,1:T(2,128)(2,1)}), bf16[2,16,2,5,2048]{4,2,3,0,1:T(2,128)(2,1)S(1)}, u32[]{:S(2)}, u32[]{:S(2)}) async-start(bf16[2,16,2,5,2048]{4,2,3,0,1:T(2,128)(2,1)} %copy.58), calls=%async_computation.3 | async-start | bytes 2621440 | tf_op jit(solution)/shard_map/all_to_all | solution.py:16
  85.0 133.9 %all-gather.6.cloned.1.call-start = ((), (), s32[]{:S(2)}) async-start(), calls=%async_computation.9 | async-start | bytes 3538944 | tf_op jit(solution)/shard_map/all_gather | solution.py:33
  142.0 12.9 %copy-start.2 = (bf16[2,16,2,5,2048]{4,2,3,0,1:T(2,128)(2,1)}, bf16[2,16,2,5,2048]{4,2,3,0,1:T(2,128)(2,1)S(1)}, u32[]{:S(2)}) copy-start(bf16[2,16,2,5,2048]{4,2,3,0,1:T(2,128)(2,1)S(1)} %all-to-all-done.3) | copy-start | bytes 3932164
  142.0 68.8 %all-to-all-start.2 = ((bf16[2,16,2,5,2048]{4,2,3,0,1:T(2,128)(2,1)}), bf16[2,16,2,5,2048]{4,2,3,0,1:T(2,128)(2,1)}, u32[]{:S(2)}, u32[]{:S(2)}) async-start(bf16[2,16,2,5,2048]{4,2,3,0,1:T(2,128)(2,1)} %copy.56), calls=%async_computation.2 | async-start | bytes 2621440 | tf_op jit(solution)/shard_map/all_to_all | solution.py:16
  154.3 102.0 %all-gather.4.cloned.1.call-start = ((), (), s32[]{:S(2)}) async-start(), calls=%async_computation.8 | async-start | bytes 3538944 | tf_op jit(solution)/shard_map/all_gather | solution.py:34
  155.0 216.9 %reduce-scatter.2.cloned.1.call-start = ((), (), s32[]{:S(2)}) async-start(), calls=%async_computation.11 | async-start | bytes 3538944 | tf_op jit(solution)/shard_map/reduce_scatter | solution.py:78
  214.3 4.6 %copy-start.4 = (bf16[320,2048]{1,0:T(8,128)(2,1)S(1)}, bf16[320,2048]{1,0:T(8,128)(2,1)}, u32[]{:S(2)}) copy-start(bf16[320,2048]{1,0:T(8,128)(2,1)} %reshape.61) | copy-start | bytes 3932164
  218.9 4.2 %copy-start.3 = (bf16[320,2048]{1,0:T(8,128)(2,1)S(1)}, bf16[320,2048]{1,0:T(8,128)(2,1)}, u32[]{:S(2)}) copy-start(bf16[320,2048]{1,0:T(8,128)(2,1)} %reshape.60) | copy-start | bytes 3932164
  218.9 4.2 %copy-start.8 = (f32[320,768]{1,0:T(8,128)S(1)}, f32[320,768]{1,0:T(8,128)}, u32[]{:S(2)}) copy-start(f32[320,768]{1,0:T(8,128)} %fusion.2) | copy-start | bytes 2949124
  222.1 0.9 copy-start.10
  226.7 32.8 %copy-start.9 = (f32[320,768]{1,0:T(8,128)S(1)}, f32[320,768]{1,0:T(8,128)}, u32[]{:S(2)}) copy-start(f32[320,768]{1,0:T(8,128)} %fusion.2) | copy-start | bytes 2949124
  256.3 3.2 copy-start.6
  256.3 3.2 copy-start.11
  259.5 1.9 copy-start.7
  367.1 4.8 %copy-start.1 = (bf16[128,2048]{1,0:T(8,128)(2,1)S(1)}, bf16[128,2048]{1,0:T(8,128)(2,1)}, u32[]{:S(2)}) copy-start(bf16[128,2048]{1,0:T(8,128)(2,1)} %param.8) | copy-start | bytes 1572868
Sparse Core Ops, SparseCore 0:
  11.2 85.0 all-gather.7
  99.4 76.5 all-gather.5
  179.2 77.0 all-gather.3
  261.5 94.4 reduce-scatter.1
where the time goes:
time: 379 us; the launch traced here: 378 us
  blocking collectives  143 us (38%)
  waiting for transfers between devices  138 us (36%)
  local copies, waits for them, and re-layouts  30.6 us (8%)
  starting transfers between devices  24.7 us (7%)
  matrix products  24 us (6%)
  between operations  14 us (4%)
  other arithmetic  4.2 us (1%)
    all_to_all x2, waiting for transfers between devices, local_then_z(): return [lax.all_to_all(x[k], 'z', 1, 1, tiled=True) for k in range(kinds)]  106 us
    all_to_all x1, blocking collectives, z_then_local(): x = lax.all_to_all(x, 'z', 1, 1, tiled=True)  74.4 us
    all_to_all x1, blocking collectives, local_then_z(): x = lax.all_to_all(x, 'ylo', 1, 1, tiled=True)  38.4 us
    all_gather x1, waiting for transfers between devices, body(): w_down = lax.all_gather(down_weight, 'dp', axis=1, tiled=True)[0]  29.6 us
    all_to_all x2, starting transfers between devices, local_then_z(): return [lax.all_to_all(x[k], 'z', 1, 1, tiled=True) for k in range(kinds)]  24.4 us
    all_to_all x1, blocking collectives, z_then_local(): x = lax.all_to_all(x, 'ylo', 0, 0, tiled=True)  17.1 us
  transfers between devices with their start and end apart: 6, of which 3 were waited for; matrix products, arithmetic and copies ran while one was open for 15% of the time, Pallas kernels for 0%

commit v1 on v0

--- a/solution.py
+++ b/solution.py
@@ -8,6 +8,13 @@
 CAP = 5
 SUB = ("ylo", "z", "core")
 ROWS = ("dp",) + SUB
+
+
+def gather_over(x, name, dim):
+    devices = lax.axis_size(name)
+    blocks = jnp.stack([x for _ in range(devices)])
+    blocks = lax.all_to_all(blocks, name, split_axis=0, concat_axis=0)
+    return jnp.concatenate(blocks, axis=dim)
 
 
 def local_then_z(x, kinds):
@@ -31,7 +38,7 @@
     positions = expert_count * capacity
     w_gate = lax.all_gather(gate_weight, "dp", axis=1, tiled=True)[0]
     w_up = lax.all_gather(up_weight, "dp", axis=1, tiled=True)[0]
-    w_down = lax.all_gather(down_weight, "dp", axis=1, tiled=True)[0]
+    w_down = gather_over(down_weight, "dp", 1)[0]
     flat_ids = expert_ids.reshape(-1)
     onehot = (flat_ids[:, None] == jnp.arange(expert_count, dtype=jnp.int32)[None, :]).astype(
         jnp.int32

time: 379 us -> 410 us (1.082)
  waiting for transfers between devices: 138 us -> 159 us
  starting transfers between devices: 24.7 us -> 33.9 us
  blocking collectives: 143 us -> 137 us
    all_to_all x0 -> x1, waiting for transfers between devices: none -> 38.5 us  [gather_over(): blocks = lax.all_to_all(blocks, name, split_axis=0, concat_axis=0)]
    all_gather x1 -> x0, waiting for transfers between devices: 29.6 us -> none  [body(): w_down = lax.all_gather(down_weight, 'dp', axis=1, tiled=True)[0]]
    all_gather x1, waiting for transfers between devices: 0.01 us -> 9.5 us  [body(): w_up = lax.all_gather(up_weight, 'dp', axis=1, tiled=True)[0]]
    all_to_all x0 -> x1, starting transfers between devices: none -> 6.63 us  [gather_over(): blocks = lax.all_to_all(blocks, name, split_axis=0, concat_axis=0)]
    all_to_all x1, blocking collectives: 38.4 us -> 32.7 us  [local_then_z(): x = lax.all_to_all(x, 'ylo', 1, 1, tiled=True)]
  transfers between devices with their start and end apart: 6 -> 6, of which waited for: 3 -> 4; matrix products, arithmetic and copies ran while one was open for 15% -> 9% of each run, Pallas kernels for 0% -> 0%
where the time goes in v1:
time: 410 us; the launch traced here: 409 us
  waiting for transfers between devices  159 us (39%)
  blocking collectives  137 us (33%)
  local copies, waits for them, and re-layouts  34 us (8%)
  starting transfers between devices  33.9 us (8%)
  matrix products  27 us (7%)
  between operations  13.9 us (3%)
  other arithmetic  4.2 us (1%)
    all_to_all x2, waiting for transfers between devices, local_then_z(): return [lax.all_to_all(x[k], 'z', 1, 1, tiled=True) for k in range(kinds)]  110 us
    all_to_all x1, blocking collectives, z_then_local(): x = lax.all_to_all(x, 'z', 1, 1, tiled=True)  74.1 us
    all_to_all x1, waiting for transfers between devices, gather_over(): blocks = lax.all_to_all(blocks, name, split_axis=0, concat_axis=0)  38.5 us
    all_to_all x1, blocking collectives, local_then_z(): x = lax.all_to_all(x, 'ylo', 1, 1, tiled=True)  32.7 us
    all_to_all x2, starting transfers between devices, local_then_z(): return [lax.all_to_all(x[k], 'z', 1, 1, tiled=True) for k in range(kinds)]  27 us
    all_to_all x1, blocking collectives, z_then_local(): x = lax.all_to_all(x, 'ylo', 0, 0, tiled=True)  17.1 us
    all_gather x1, waiting for transfers between devices, body(): w_up = lax.all_gather(up_weight, 'dp', axis=1, tiled=True)[0]  9.5 us
  transfers between devices with their start and end apart: 6, of which 4 were waited for; matrix products, arithmetic and copies ran while one was open for 9% of the time, Pallas kernels for 0%

profile of v1, /device:TPU:33, one launch (start us, length us, event | category | flops | bytes accessed | tf_op | source)
XLA Modules:
  0.0 409.2 jit_solution(7696508327362618709)
XLA Ops:
  12.9 2.4 stack.9
  16.9 3.4 stack.8
  20.3 2.5 pad_maximum_fusion
  24.6 6.1 %all_to_all.40 = bf16[2,2,16,2,5,2048]{5,2,4,1,0,3:T(8,128)(2,1)S(1)} all-to-all(bf16[2,2,16,2,5,2048]{5,2,4,1,0,3:T(8,128)(2,1)S(1)} %copy.54), channel_id=1, replica_groups=mesh['dp'=8,'ylo'=2,'z'=16,'core'=2] {'core'}, dimensions={3} | all-to-all | bytes 5242880 | tf_op jit(solution)/shard_map/all_to_all | solution.py:21
  31.0 32.7 %all_to_all.41 = bf16[2,2,16,2,5,2048]{5,2,4,3,0,1:T(8,128)(2,1)S(1)} all-to-all(bf16[2,2,16,2,5,2048]{5,2,4,3,0,1:T(8,128)(2,1)S(1)} %copy.55), channel_id=1, replica_groups=mesh['dp'=8,'ylo'=2,'z'=16,'core'=2] {'ylo'}, dimensions={1} | all-to-all | bytes 5242880 | tf_op jit(solution)/shard_map/all_to_all | solution.py:22
  64.0 2.4 copy.58
  66.5 14.6 %all-to-all-start.4 = ((bf16[2,16,2,5,2048]{4,2,3,0,1:T(2,128)(2,1)}), bf16[2,16,2,5,2048]{4,2,3,0,1:T(2,128)(2,1)S(1)}, u32[]{:S(2)}, u32[]{:S(2)}) async-start(bf16[2,16,2,5,2048]{4,2,3,0,1:T(2,128)(2,1)} %copy.58), calls=%async_computation.4 | async-start | bytes 2621440 | tf_op jit(solution)/shard_map/all_to_all | solution.py:23
  81.8 2.4 copy.56
  84.3 53.9 %all-to-all-done.4 = bf16[2,16,2,5,2048]{4,2,3,0,1:T(2,128)(2,1)S(1)} async-done(((bf16[2,16,2,5,2048]{4,2,3,0,1:T(2,128)(2,1)}), bf16[2,16,2,5,2048]{4,2,3,0,1:T(2,128)(2,1)S(1)}, u32[]{:S(2)}, u32[]{:S(2)}) %all-to-all-start.4) | async-done | bytes 1310752 | tf_op jit(solution)/shard_map/all_to_all | solution.py:23
  138.2 12.3 %all-to-all-start.2 = ((bf16[2,16,2,5,2048]{4,2,3,0,1:T(2,128)(2,1)}), bf16[2,16,2,5,2048]{4,2,3,0,1:T(2,128)(2,1)S(1)}, u32[]{:S(2)}, u32[]{:S(2)}) async-start(bf16[2,16,2,5,2048]{4,2,3,0,1:T(2,128)(2,1)} %copy.56), calls=%async_computation.2 | async-start | bytes 2621440 | tf_op jit(solution)/shard_map/all_to_all | solution.py:23
  151.2 55.7 %all-to-all-done.2 = bf16[2,16,2,5,2048]{4,2,3,0,1:T(2,128)(2,1)S(1)} async-done(((bf16[2,16,2,5,2048]{4,2,3,0,1:T(2,128)(2,1)}), bf16[2,16,2,5,2048]{4,2,3,0,1:T(2,128)(2,1)S(1)}, u32[]{:S(2)}, u32[]{:S(2)}) %all-to-all-start.2) | async-done | bytes 1310752 | tf_op jit(solution)/shard_map/all_to_all | solution.py:23
  209.0 6.6 %all-to-all-start.3 = ((bf16[8,1,256,768]{3,2,1,0:T(8,128)(2,1)}), bf16[8,1,256,768]{3,2,1,0:T(8,128)(2,1)}, u32[]{:S(2)}, u32[]{:S(2)}) async-start(bf16[8,1,256,768]{3,2,1,0:T(8,128)(2,1)} %stack.11), calls=%async_computation.3 | async-start | bytes 6291456 | tf_op jit(solution)/shard_map/all_to_all | solution.py:16
  223.0 38.5 %all-to-all-done.3 = bf16[8,1,256,768]{3,2,1,0:T(8,128)(2,1)} async-done(((bf16[8,1,256,768]{3,2,1,0:T(8,128)(2,1)}), bf16[8,1,256,768]{3,2,1,0:T(8,128)(2,1)}, u32[]{:S(2)}, u32[]{:S(2)}) %all-to-all-start.3) | async-done | bytes 3145760 | tf_op jit(solution)/shard_map/all_to_all | solution.py:16
  261.6 4.5 %fusion.29 = f32[320,768]{1,0:T(8,128)} fusion(bf16[320,2048]{1,0:T(8,128)(2,1)} %reshape.63, bf16[2048,768]{1,0:T(8,128)(2,1)} %bitcast.3), kind=kOutput, calls=%fused_computation.45 | convolution fusion | flops 1006632960 | bytes 5439488 | tf_op jit(solution)/shard_map/dot_general | solution.py:68
  266.1 4.0 fusion.2
  270.1 9.5 %all-gather.3.cloned.1.call-done = bf16[1,2048,768]{2,1,0:T(8,128)(2,1)} async-done(((bf16[1,256,768]{2,1,0:T(8,128)(2,1)}), bf16[1,2048,768]{2,1,0:T(8,128)(2,1)}) %all-gather.3.cloned.1.call-update) | async-done | bytes 3145744 | tf_op jit(solution)/shard_map/all_gather | solution.py:40
  279.6 3.1 fusion.6
  283.7 3.7 convolution_convert_fusion
  288.9 3.6 fusion
  294.9 2.4 reshape.65
  298.8 74.1 %all_to_all.42 = bf16[2,16,2,5,2048]{4,2,3,0,1:T(2,128)(2,1)S(1)} all-to-all(bf16[2,16,2,5,2048]{4,2,3,0,1:T(2,128)(2,1)S(1)} %copy.60), channel_id=1, replica_groups=mesh['dp'=8,'ylo'=2,'z'=16,'core'=2] {'z'}, dimensions={1} | all-to-all | bytes 2621440 | tf_op jit(solution)/shard_map/all_to_all | solution.py:27
  373.6 17.1 %all_to_all.43 = bf16[2,16,2,5,2048]{4,1,3,2,0:T(8,128)(2,1)S(1)} all-to-all(bf16[2,16,2,5,2048]{4,1,3,2,0:T(8,128)(2,1)S(1)} %copy.61), channel_id=1, replica_groups=mesh['dp'=8,'ylo'=2,'z'=16,'core'=2] {'ylo'}, dimensions={0} | all-to-all | bytes 2621440 | tf_op jit(solution)/shard_map/all_to_all | solution.py:28
  390.8 7.2 %all_to_all.44 = bf16[2,16,2,5,2048]{4,1,3,0,2:T(8,128)(2,1)S(1)} all-to-all(bf16[2,16,2,5,2048]{4,1,3,0,2:T(8,128)(2,1)S(1)} %copy.62), channel_id=1, replica_groups=mesh['dp'=8,'ylo'=2,'z'=16,'core'=2] {'core'}, dimensions={2} | all-to-all | bytes 2621440 | tf_op jit(solution)/shard_map/all_to_all | solution.py:29
  400.1 2.6 convolution_convert_fusion.2
  (67 shorter events, 29.7 us)
Async XLA Ops:
  7.2 4.2 %copy-start = (bf16[128,2048]{1,0:T(8,128)(2,1)S(1)}, bf16[128,2048]{1,0:T(8,128)(2,1)}, u32[]{:S(2)}) copy-start(bf16[128,2048]{1,0:T(8,128)(2,1)} %param.8) | copy-start | bytes 1572868
  12.9 2.4 copy-start.6
  66.5 71.7 %all-to-all-start.4 = ((bf16[2,16,2,5,2048]{4,2,3,0,1:T(2,128)(2,1)}), bf16[2,16,2,5,2048]{4,2,3,0,1:T(2,128)(2,1)S(1)}, u32[]{:S(2)}, u32[]{:S(2)}) async-start(bf16[2,16,2,5,2048]{4,2,3,0,1:T(2,128)(2,1)} %copy.58), calls=%async_computation.4 | async-start | bytes 2621440 | tf_op jit(solution)/shard_map/all_to_all | solution.py:23
  81.1 184.9 %all-gather.5.cloned.1.call-start = ((), (), s32[]{:S(2)}) async-start(), calls=%async_computation.10 | async-start | bytes 3538944 | tf_op jit(solution)/shard_map/all_gather | solution.py:39
  84.3 122.7 %copy-start.7 = (bf16[1,256,768]{2,1,0:T(8,128)(2,1)S(1)}, bf16[1,256,768]{2,1,0:T(8,128)(2,1)}, u32[]{:S(2)}) copy-start(bf16[1,256,768]{2,1,0:T(8,128)(2,1)} %param.13) | copy-start | bytes 1179652
  138.2 70.8 %copy-start.2 = (bf16[2,16,2,5,2048]{4,2,3,0,1:T(2,128)(2,1)}, bf16[2,16,2,5,2048]{4,2,3,0,1:T(2,128)(2,1)S(1)}, u32[]{:S(2)}) copy-start(bf16[2,16,2,5,2048]{4,2,3,0,1:T(2,128)(2,1)S(1)} %all-to-all-done.4) | copy-start | bytes 3932164
  138.2 68.8 %all-to-all-start.2 = ((bf16[2,16,2,5,2048]{4,2,3,0,1:T(2,128)(2,1)}), bf16[2,16,2,5,2048]{4,2,3,0,1:T(2,128)(2,1)S(1)}, u32[]{:S(2)}, u32[]{:S(2)}) async-start(bf16[2,16,2,5,2048]{4,2,3,0,1:T(2,128)(2,1)} %copy.56), calls=%async_computation.2 | async-start | bytes 2621440 | tf_op jit(solution)/shard_map/all_to_all | solution.py:23
  150.5 129.1 %all-gather.3.cloned.1.call-start = ((), (), s32[]{:S(2)}) async-start(), calls=%async_computation.9 | async-start | bytes 3538944 | tf_op jit(solution)/shard_map/all_gather | solution.py:40
  207.0 2.0 copy-start.3
  209.0 52.5 %all-to-all-start.3 = ((bf16[8,1,256,768]{3,2,1,0:T(8,128)(2,1)}), bf16[8,1,256,768]{3,2,1,0:T(8,128)(2,1)}, u32[]{:S(2)}, u32[]{:S(2)}) async-start(bf16[8,1,256,768]{3,2,1,0:T(8,128)(2,1)} %stack.11), calls=%async_computation.3 | async-start | bytes 6291456 | tf_op jit(solution)/shard_map/all_to_all | solution.py:16
  215.7 187.1 %reduce-scatter.2.cloned.1.call-start = ((), (), s32[]{:S(2)}) async-start(), calls=%async_computation.11 | async-start | bytes 3538944 | tf_op jit(solution)/shard_map/reduce_scatter | solution.py:85
  261.5 4.5 %copy-start.4 = (bf16[320,2048]{1,0:T(8,128)(2,1)S(1)}, bf16[320,2048]{1,0:T(8,128)(2,1)}, u32[]{:S(2)}) copy-start(bf16[320,2048]{1,0:T(8,128)(2,1)} %reshape.64) | copy-start | bytes 3932164
  270.1 13.6 %copy-start.5 = (bf16[320,2048]{1,0:T(8,128)(2,1)S(1)}, bf16[320,2048]{1,0:T(8,128)(2,1)}, u32[]{:S(2)}) copy-start(bf16[320,2048]{1,0:T(8,128)(2,1)} %reshape.63) | copy-start | bytes 3932164
  279.6 4.1 %copy-start.10 = (f32[320,768]{1,0:T(8,128)S(1)}, f32[320,768]{1,0:T(8,128)}, u32[]{:S(2)}) copy-start(f32[320,768]{1,0:T(8,128)} %fusion.2) | copy-start | bytes 2949124
  282.8 1.0 copy-start.12
  287.4 1.2 copy-start.9
  287.4 1.5 copy-start.11
  288.9 3.7 copy-start.8
  398.0 4.8 %copy-start.1 = (bf16[128,2048]{1,0:T(8,128)(2,1)S(1)}, bf16[128,2048]{1,0:T(8,128)(2,1)}, u32[]{:S(2)}) copy-start(bf16[128,2048]{1,0:T(8,128)(2,1)} %param.8) | copy-start | bytes 1572868
Sparse Core Ops, SparseCore 0:
  85.1 80.1 all-gather.4
  168.5 111.0 all-gather.2
  287.5 91.9 reduce-scatter.1
